TPU v7x, 512 devices: a whole 4x4x16 slice. The times are simulated.
512 devices in a mesh: outer: 16 (over z), inner: 32 (over y, x, core).
Axes of the slice: x: 4, y: 4, z: 16, core: 2. Of those that a mesh axis runs over, the one named last changes fastest.
Arguments:
- field_slab: float32 [512, 128, 4096], P(None, 'inner', 'outer'), may hold values from -48 to 48, as said below
- start_block: float32 [512, 256], replicated, may hold values from -6 to 6
Outputs:
- factor: float32 [512, 256], replicated
- core_fibres: float32 [256, 128, 4096], P('inner', None, 'outer')
Inputs may be any that keep to these rules, and one draw needn't show every extreme that they name: `field_slab`: real values.
All inputs are finite; a program needn't handle non-finite values.
Results may differ from a plain program's by a relative error of at most 0.00016.
Values sent between devices are 32-bit elements; how exact they have to be, the bound alone decides.
No kernel may reach another device: no remote copies, remote signals or barrier semaphores. Data moves between devices by JAX's collectives and lax.ppermute only.
A program may use at most 64 MiB of HBM per device.

v0:
```python
import jax
import jax.numpy as jnp
from jax import lax
from jax.sharding import PartitionSpec as P

ITERS = 2


def product(first_mat, second_mat):
    return jnp.dot(
        first_mat, second_mat, precision=lax.Precision.HIGHEST, preferred_element_type=jnp.float32
    )


def orthonormal(block):
    chol_factor = jnp.linalg.cholesky(product(block.T, block))
    return lax.linalg.triangular_solve(
        chol_factor, block, left_side=False, lower=True, transpose_a=True
    )


def on_device(field_slab, start_block):
    order_rows = field_slab.shape[0]
    local_shape = field_slab.shape
    unfolded = field_slab.reshape(order_rows, local_shape[1] * local_shape[2])
    gram_local = product(unfolded, unfolded.T)
    subspace = orthonormal(start_block)
    gram_total = lax.psum(gram_local, ("outer", "inner"))
    for sweep_index in range(ITERS):
        subspace = orthonormal(product(gram_total, subspace))
    core_block = product(subspace.T, unfolded).reshape(
        subspace.shape[1], local_shape[1], local_shape[2]
    )
    core_fibres = lax.all_to_all(core_block, "inner", split_axis=0, concat_axis=1, tiled=True)
    return (subspace, core_fibres)


def solution(mesh):
    in_specs = (P(None, "inner", "outer"), P())
    out_specs = (P(), P("inner", None, "outer"))
    return jax.shard_map(
        on_device, mesh=mesh, in_specs=in_specs, out_specs=out_specs, check_vma=False
    )
```

profile of v0, /device:TPU:1, one launch (start us, length us, event | category | flops | bytes accessed | tf_op | source)
XLA Modules:
  0.0 663.9 jit_solution(16527323154972641272)
XLA Ops:
  7.2 7.2 %fusion.2 = f32[512,512]{1,0:T(8,128)} fusion(f32[512,4,256]{2,1,0:T(4,128)} %param.5), kind=kOutput, calls=%fused_computation.8 | convolution fusion | flops 3221225472 | bytes 3145728 | tf_op jit(solution)/shard_map/dot_general | solution.py:10
  14.4 1.0 fusion.52
  15.7 11.7 %cholesky.172 = f32[128,128]{1,0:T(8,128)S(1)} custom-call(f32[128,128]{1,0:T(8,128)S(1)} %cholesky.270), custom_call_target="Cholesky" | custom-call | tf_op jit(solution)/shard_map/jit(cholesky)/cholesky | solution.py:16
  27.4 9.8 %custom-call.15 = f32[1,128,128]{1,2,0:T(8,128)S(1)} custom-call(f32[1,128,128]{2,1,0:T(8,128)S(1)} %get-tuple-element.72), custom_call_target="InvertDiagBlocksLowerTriangular" | custom-call | tf_op jit(solution)/shard_map/jit(cholesky)/cholesky | solution.py:16
  37.7 12.0 %cholesky.189 = f32[128,128]{1,0:T(8,128)S(1)} custom-call(f32[128,128]{1,0:T(8,128)S(1)} %convolution_subtract_fusion.5), custom_call_target="Cholesky" | custom-call | tf_op jit(solution)/shard_map/jit(cholesky)/cholesky | solution.py:16
  49.7 0.7 compare_reduce_fusion.4
  51.7 3.8 while.6
  52.3 1.3 bitcast_dynamic-update-slice_fusion.6
  54.2 1.3 bitcast_dynamic-update-slice_fusion.6
  55.5 19.7 %custom-call.16 = f32[2,128,128]{1,2,0:T(8,128)S(1)} custom-call(f32[2,128,128]{2,1,0:T(8,128)S(1)} %get-tuple-element.24), custom_call_target="InvertDiagBlocksLowerTriangular" | custom-call | tf_op jit(solution)/shard_map/triangular_solve/custom-call.0 | solution.py:17
  75.6 1.8 copy.21
  77.4 1.9 copy.17
  79.4 0.6 convolution_subtract_fusion.2
  80.4 406.9 %all-reduce.3.cloned.1.call-done = f32[512,512]{1,0:T(8,128)} async-done(((f32[512,512]{1,0:T(8,128)}), f32[512,512]{1,0:T(8,128)}) %all-reduce.3.cloned.1.call-update) | async-done | bytes 1048592 | tf_op jit(solution)/shard_map/psum | solution.py:28
  487.3 2.2 fusion.5
  489.5 1.0 fusion.53
  490.8 11.7 %cholesky.206 = f32[128,128]{1,0:T(8,128)S(1)} custom-call(f32[128,128]{1,0:T(8,128)S(1)} %cholesky.273), custom_call_target="Cholesky" | custom-call | tf_op jit(solution)/shard_map/jit(cholesky)/cholesky | solution.py:16
  502.5 9.8 %custom-call.17 = f32[1,128,128]{1,2,0:T(8,128)S(1)} custom-call(f32[1,128,128]{2,1,0:T(8,128)S(1)} %get-tuple-element.68), custom_call_target="InvertDiagBlocksLowerTriangular" | custom-call | tf_op jit(solution)/shard_map/jit(cholesky)/cholesky | solution.py:16
  512.8 22.6 %cholesky.223 = f32[128,128]{1,0:T(8,128)S(1)} custom-call(f32[128,128]{1,0:T(8,128)S(1)} %convolution_subtract_fusion.4), custom_call_target="Cholesky" | custom-call | tf_op jit(solution)/shard_map/jit(cholesky)/cholesky | solution.py:16
  535.5 0.7 compare_reduce_fusion.2
  536.2 0.6 compare_reduce_fusion.3
  538.2 4.1 while.7
  538.3 0.6 fusion.80
  538.9 1.4 bitcast_dynamic-update-slice_fusion.7
  540.3 0.6 fusion.80
  540.9 1.4 bitcast_dynamic-update-slice_fusion.7
  542.4 19.7 %custom-call.18 = f32[2,128,128]{1,2,0:T(8,128)S(1)} custom-call(f32[2,128,128]{2,1,0:T(8,128)S(1)} %get-tuple-element.25), custom_call_target="InvertDiagBlocksLowerTriangular" | custom-call | tf_op jit(solution)/shard_map/triangular_solve/custom-call.0 | solution.py:17
  562.5 0.6 convolution_subtract_fusion.1
  563.5 1.0 fusion.9
  564.5 1.0 fusion.54
  565.8 11.7 %cholesky.240 = f32[128,128]{1,0:T(8,128)S(1)} custom-call(f32[128,128]{1,0:T(8,128)S(1)} %cholesky.276), custom_call_target="Cholesky" | custom-call | tf_op jit(solution)/shard_map/jit(cholesky)/cholesky | solution.py:16
  577.5 9.8 %custom-call.19 = f32[1,128,128]{1,2,0:T(8,128)S(1)} custom-call(f32[1,128,128]{2,1,0:T(8,128)S(1)} %get-tuple-element.64), custom_call_target="InvertDiagBlocksLowerTriangular" | custom-call | tf_op jit(solution)/shard_map/jit(cholesky)/cholesky | solution.py:16
  587.8 11.9 %cholesky.257 = f32[128,128]{1,0:T(8,128)S(1)} custom-call(f32[128,128]{1,0:T(8,128)S(1)} %convolution_subtract_fusion.3), custom_call_target="Cholesky" | custom-call | tf_op jit(solution)/shard_map/jit(cholesky)/cholesky | solution.py:16
  599.8 0.7 compare_reduce_fusion
  600.5 0.6 compare_reduce_fusion.1
  602.5 4.1 while.8
  602.5 0.6 fusion.81
  603.1 1.4 bitcast_dynamic-update-slice_fusion.8
  604.6 0.6 fusion.81
  605.2 1.4 bitcast_dynamic-update-slice_fusion.8
  606.6 19.7 %custom-call.20 = f32[2,128,128]{1,2,0:T(8,128)S(1)} custom-call(f32[2,128,128]{2,1,0:T(8,128)S(1)} %get-tuple-element.26), custom_call_target="InvertDiagBlocksLowerTriangular" | custom-call | tf_op jit(solution)/shard_map/triangular_solve/custom-call.0 | solution.py:17
  626.7 0.6 convolution_subtract_fusion
  627.8 1.9 fusion.13
  629.7 1.6 copy.18
  631.3 6.6 %all-to-all-start = ((f32[256,4,256]{2,1,0:T(4,128)}), f32[256,4,256]{2,1,0:T(4,128)S(1)}, u32[]{:S(2)}, u32[]{:S(2)}) async-start(f32[256,4,256]{2,1,0:T(4,128)} %copy.18), calls=%async_computation | async-start | bytes 2097152 | tf_op jit(solution)/shard_map/all_to_all | solution.py:34
  638.0 1.0 copy.20
  639.0 16.1 %all-to-all-done = f32[256,4,256]{2,1,0:T(4,128)S(1)} async-done(((f32[256,4,256]{2,1,0:T(4,128)}), f32[256,4,256]{2,1,0:T(4,128)S(1)}, u32[]{:S(2)}, u32[]{:S(2)}) %all-to-all-start) | async-done | bytes 1048608 | tf_op jit(solution)/shard_map/all_to_all | solution.py:34
  655.4 1.3 all_to_all.16
  (56 shorter events, 6.4 us)
Async XLA Ops:
  7.2 7.2 %copy-start = (f32[512,256]{1,0:T(8,128)S(1)}, f32[512,256]{1,0:T(8,128)}, u32[]{:S(2)}) copy-start(f32[512,256]{1,0:T(8,128)} %param.6) | copy-start | bytes 1572868
  7.2 480.1 %all-reduce.3.cloned.1.call-start = ((), (), s32[]{:S(2)}) async-start(), calls=%async_computation.1 | async-start | bytes 2097152 | tf_op jit(solution)/shard_map/psum | solution.py:28
  15.6 60.0 %copy-start.2 = (f32[512,4,256]{2,1,0:T(4,128)S(1)}, f32[512,4,256]{2,1,0:T(4,128)}, u32[]{:S(2)}) copy-start(f32[512,4,256]{2,1,0:T(4,128)} %param.5) | copy-start | bytes 6291460
  562.0 1.4 copy-start.1
  631.3 23.8 %all-to-all-start = ((f32[256,4,256]{2,1,0:T(4,128)}), f32[256,4,256]{2,1,0:T(4,128)S(1)}, u32[]{:S(2)}, u32[]{:S(2)}) async-start(f32[256,4,256]{2,1,0:T(4,128)} %copy.18), calls=%async_computation | async-start | bytes 2097152 | tf_op jit(solution)/shard_map/all_to_all | solution.py:34
Sparse Core Ops, SparseCore 0:
  14.5 472.7 all-reduce.2
where the time goes:
time: 673 us; the launch traced here: 664 us
  waiting for transfers between devices  423 us (63%)
  other arithmetic  174 us (26%)
  matrix products  21.1 us (3%)
  local copies, waits for them, and re-layouts  20.3 us (3%)
  between operations  18.7 us (3%)
    psum x1, waiting for transfers between devices, on_device(): gram_total = lax.psum(gram_local, ('outer', 'inner'))  407 us
    another operation x20, other arithmetic, orthonormal(): chol_factor = jnp.linalg.cholesky(product(block.T, block))  115 us
    another operation x8, other arithmetic, orthonormal(): lax.linalg.triangular_solve(chol_factor, block, left_side=False, lower=Tr...  59.2 us
    all_to_all x1, waiting for transfers between devices, on_device(): lax.all_to_all(core_block, 'inner', split_axis=0, concat_axis=1, tiled=True)  16.1 us
    dot_general x7, matrix products, product(): jnp.dot(first_mat, second_mat, precision=lax.Precision.HIGHEST, preferred...  15.4 us
  transfers between devices with their start and end apart: 2, of which 2 were waited for; matrix products, arithmetic and copies ran while one was open for 10% of the time, Pallas kernels for 0%

commit v1 on v0

--- a/solution.py
+++ b/solution.py
@@ -25,7 +25,10 @@
     unfolded = field_slab.reshape(order_rows, local_shape[1] * local_shape[2])
     gram_local = product(unfolded, unfolded.T)
     subspace = orthonormal(start_block)
-    gram_total = lax.psum(gram_local, ("outer", "inner"))
+    close_ways_here = lambda x_local, row_axis, axis_name: lax.psum(
+        lax.psum(x_local, axis_name=row_axis), axis_name=axis_name
+    )
+    gram_total = close_ways_here(gram_local, "outer", axis_name="inner")
     for sweep_index in range(ITERS):
         subspace = orthonormal(product(gram_total, subspace))
     core_block = product(subspace.T, unfolded).reshape(

time: 673 us -> 464 us (0.69)
  waiting for transfers between devices: 423 us -> 231 us
  other arithmetic: 174 us -> 163 us
    psum x1 -> x2, waiting for transfers between devices: 407 us -> 214 us  [the longest x1 140 us: on_device(): lax.psum(lax.psum(x_local, axis_name=row_axis), axis_name=axis_name)]
    another operation x20, other arithmetic: 115 us -> 104 us  [orthonormal(): chol_factor = jnp.linalg.cholesky(product(block.T, block))]
  transfers between devices with their start and end apart: 2 -> 3, of which waited for: 2 -> 3; matrix products, arithmetic and copies ran while one was open for 10% -> 14% of each run, Pallas kernels for 0% -> 0%
where the time goes in v1:
time: 464 us; the launch traced here: 460 us
  waiting for transfers between devices  231 us (50%)
  other arithmetic  163 us (35%)
  matrix products  21.1 us (5%)
  local copies, waits for them, and re-layouts  20.3 us (4%)
  between operations  18.5 us (4%)
  starting transfers between devices  6.31 us (1%)
    psum x1, waiting for transfers between devices, on_device(): lax.psum(lax.psum(x_local, axis_name=row_axis), axis_name=axis_name)  140 us
    another operation x20, other arithmetic, orthonormal(): chol_factor = jnp.linalg.cholesky(product(block.T, block))  104 us
    psum x1, waiting for transfers between devices, on_device(): lax.psum(x_local, axis_name=row_axis)  74.3 us
    another operation x8, other arithmetic, orthonormal(): lax.linalg.triangular_solve(chol_factor, block, left_side=False, lower=Tr...  59.2 us
    all_to_all x1, waiting for transfers between devices, on_device(): lax.all_to_all(core_block, 'inner', split_axis=0, concat_axis=1, tiled=True)  16.1 us
    dot_general x7, matrix products, product(): jnp.dot(first_mat, second_mat, precision=lax.Precision.HIGHEST, preferred...  15.4 us
    another operation x22, local copies, waits for them, and re-layouts, orthonormal(): lax.linalg.triangular_solve(chol_factor, block, left_side=False, lower=Tr...  11.9 us
  transfers between devices with their start and end apart: 3, of which 3 were waited for; matrix products, arithmetic and copies ran while one was open for 14% of the time, Pallas kernels for 0%

profile of v1, /device:TPU:1, one launch (start us, length us, event | category | flops | bytes accessed | tf_op | source)
XLA Modules:
  0.0 460.1 jit_solution(6431365954701264129)
XLA Ops:
  7.2 7.2 %fusion.2 = f32[512,512]{1,0:T(8,128)} fusion(f32[512,4,256]{2,1,0:T(4,128)} %param.5), kind=kOutput, calls=%fused_computation.8 | convolution fusion | flops 3221225472 | bytes 3145728 | tf_op jit(solution)/shard_map/dot_general | solution.py:10
  14.6 1.0 fusion.52
  15.9 11.7 %cholesky.172 = f32[128,128]{1,0:T(8,128)S(1)} custom-call(f32[128,128]{1,0:T(8,128)S(1)} %cholesky.270), custom_call_target="Cholesky" | custom-call | tf_op jit(solution)/shard_map/jit(cholesky)/cholesky | solution.py:16
  27.6 9.8 %custom-call.15 = f32[1,128,128]{1,2,0:T(8,128)S(1)} custom-call(f32[1,128,128]{2,1,0:T(8,128)S(1)} %get-tuple-element.72), custom_call_target="InvertDiagBlocksLowerTriangular" | custom-call | tf_op jit(solution)/shard_map/jit(cholesky)/cholesky | solution.py:16
  37.9 11.7 %cholesky.189 = f32[128,128]{1,0:T(8,128)S(1)} custom-call(f32[128,128]{1,0:T(8,128)S(1)} %convolution_subtract_fusion.5), custom_call_target="Cholesky" | custom-call | tf_op jit(solution)/shard_map/jit(cholesky)/cholesky | solution.py:16
  49.7 0.7 compare_reduce_fusion.4
  51.7 4.2 while.6
  52.7 1.3 bitcast_dynamic-update-slice_fusion.6
  54.6 1.3 bitcast_dynamic-update-slice_fusion.6
  55.9 19.7 %custom-call.16 = f32[2,128,128]{1,2,0:T(8,128)S(1)} custom-call(f32[2,128,128]{2,1,0:T(8,128)S(1)} %get-tuple-element.24), custom_call_target="InvertDiagBlocksLowerTriangular" | custom-call | tf_op jit(solution)/shard_map/triangular_solve/custom-call.0 | solution.py:17
  75.6 74.3 %all-reduce.4.cloned.1.call-done = f32[512,512]{1,0:T(8,128)} async-done(((f32[512,512]{1,0:T(8,128)}), f32[512,512]{1,0:T(8,128)}) %all-reduce.4.cloned.1.call-update) | async-done | bytes 1048592 | tf_op jit(solution)/shard_map/psum | solution.py:29
  150.3 1.8 copy.21
  152.1 1.9 copy.17
  154.0 0.6 convolution_subtract_fusion.2
  155.1 140.1 %all-reduce.6.cloned.1.call-done = f32[512,512]{1,0:T(8,128)} async-done(((f32[512,512]{1,0:T(8,128)}), f32[512,512]{1,0:T(8,128)}) %all-reduce.6.cloned.1.call-update) | async-done | bytes 1048592 | tf_op jit(solution)/shard_map/psum | solution.py:28
  295.1 2.2 fusion.5
  297.4 1.0 fusion.53
  298.6 11.7 %cholesky.206 = f32[128,128]{1,0:T(8,128)S(1)} custom-call(f32[128,128]{1,0:T(8,128)S(1)} %cholesky.273), custom_call_target="Cholesky" | custom-call | tf_op jit(solution)/shard_map/jit(cholesky)/cholesky | solution.py:16
  310.4 9.8 %custom-call.17 = f32[1,128,128]{1,2,0:T(8,128)S(1)} custom-call(f32[1,128,128]{2,1,0:T(8,128)S(1)} %get-tuple-element.68), custom_call_target="InvertDiagBlocksLowerTriangular" | custom-call | tf_op jit(solution)/shard_map/jit(cholesky)/cholesky | solution.py:16
  320.7 11.9 %cholesky.223 = f32[128,128]{1,0:T(8,128)S(1)} custom-call(f32[128,128]{1,0:T(8,128)S(1)} %convolution_subtract_fusion.4), custom_call_target="Cholesky" | custom-call | tf_op jit(solution)/shard_map/jit(cholesky)/cholesky | solution.py:16
  332.6 0.6 compare_reduce_fusion.2
  333.2 0.7 compare_reduce_fusion.3
  335.2 4.1 while.7
  335.3 0.7 fusion.80
  335.9 1.3 bitcast_dynamic-update-slice_fusion.7
  337.3 0.7 fusion.80
  338.0 1.3 bitcast_dynamic-update-slice_fusion.7
  339.3 19.7 %custom-call.18 = f32[2,128,128]{1,2,0:T(8,128)S(1)} custom-call(f32[2,128,128]{2,1,0:T(8,128)S(1)} %get-tuple-element.25), custom_call_target="InvertDiagBlocksLowerTriangular" | custom-call | tf_op jit(solution)/shard_map/triangular_solve/custom-call.0 | solution.py:17
  360.5 1.0 fusion.9
  361.5 1.0 fusion.54
  362.7 11.7 %cholesky.240 = f32[128,128]{1,0:T(8,128)S(1)} custom-call(f32[128,128]{1,0:T(8,128)S(1)} %cholesky.276), custom_call_target="Cholesky" | custom-call | tf_op jit(solution)/shard_map/jit(cholesky)/cholesky | solution.py:16
  374.5 9.8 %custom-call.19 = f32[1,128,128]{1,2,0:T(8,128)S(1)} custom-call(f32[1,128,128]{2,1,0:T(8,128)S(1)} %get-tuple-element.64), custom_call_target="InvertDiagBlocksLowerTriangular" | custom-call | tf_op jit(solution)/shard_map/jit(cholesky)/cholesky | solution.py:16
  384.8 11.9 %cholesky.257 = f32[128,128]{1,0:T(8,128)S(1)} custom-call(f32[128,128]{1,0:T(8,128)S(1)} %convolution_subtract_fusion.3), custom_call_target="Cholesky" | custom-call | tf_op jit(solution)/shard_map/jit(cholesky)/cholesky | solution.py:16
  396.7 0.7 compare_reduce_fusion
  397.5 0.6 compare_reduce_fusion.1
  399.5 4.1 while.8
  399.5 0.6 fusion.81
  400.1 1.4 bitcast_dynamic-update-slice_fusion.8
  401.6 0.6 fusion.81
  402.2 1.4 bitcast_dynamic-update-slice_fusion.8
  403.6 19.7 %custom-call.20 = f32[2,128,128]{1,2,0:T(8,128)S(1)} custom-call(f32[2,128,128]{2,1,0:T(8,128)S(1)} %get-tuple-element.26), custom_call_target="InvertDiagBlocksLowerTriangular" | custom-call | tf_op jit(solution)/shard_map/triangular_solve/custom-call.0 | solution.py:17
  423.7 0.6 convolution_subtract_fusion
  424.7 1.9 fusion.13
  426.7 1.6 copy.18
  428.3 6.1 %all-to-all-start = ((f32[256,4,256]{2,1,0:T(4,128)}), f32[256,4,256]{2,1,0:T(4,128)S(1)}, u32[]{:S(2)}, u32[]{:S(2)}) async-start(f32[256,4,256]{2,1,0:T(4,128)} %copy.18), calls=%async_computation | async-start | bytes 2097152 | tf_op jit(solution)/shard_map/all_to_all | solution.py:37
  434.4 1.0 copy.20
  435.4 16.1 %all-to-all-done = f32[256,4,256]{2,1,0:T(4,128)S(1)} async-done(((f32[256,4,256]{2,1,0:T(4,128)}), f32[256,4,256]{2,1,0:T(4,128)S(1)}, u32[]{:S(2)}, u32[]{:S(2)}) %all-to-all-start) | async-done | bytes 1048608 | tf_op jit(solution)/shard_map/all_to_all | solution.py:37
  451.7 1.3 all_to_all.16
  (59 shorter events, 7.2 us)
Async XLA Ops:
  7.2 7.5 %copy-start = (f32[512,256]{1,0:T(8,128)S(1)}, f32[512,256]{1,0:T(8,128)}, u32[]{:S(2)}) copy-start(f32[512,256]{1,0:T(8,128)} %param.6) | copy-start | bytes 1572868
  7.2 142.7 %all-reduce.4.cloned.1.call-start = ((), (), s32[]{:S(2)}) async-start(), calls=%async_computation.1 | async-start | bytes 2097152 | tf_op jit(solution)/shard_map/psum | solution.py:29
  14.4 280.8 %all-reduce.6.cloned.1.call-start = ((), (), s32[]{:S(2)}) async-start(), calls=%async_computation.2 | async-start | bytes 2097152 | tf_op jit(solution)/shard_map/psum | solution.py:28
  27.6 122.7 %copy-start.2 = (f32[512,4,256]{2,1,0:T(4,128)S(1)}, f32[512,4,256]{2,1,0:T(4,128)}, u32[]{:S(2)}) copy-start(f32[512,4,256]{2,1,0:T(4,128)} %param.5) | copy-start | bytes 6291460
  359.0 1.5 copy-start.1
  428.3 23.2 %all-to-all-start = ((f32[256,4,256]{2,1,0:T(4,128)}), f32[256,4,256]{2,1,0:T(4,128)S(1)}, u32[]{:S(2)}, u32[]{:S(2)}) async-start(f32[256,4,256]{2,1,0:T(4,128)} %copy.18), calls=%async_computation | async-start | bytes 2097152 | tf_op jit(solution)/shard_map/all_to_all | solution.py:37
Sparse Core Ops, SparseCore 0:
  14.5 135.2 all-reduce.3
  153.4 141.6 all-reduce.5
